TPU v7x, 512 devices: a whole 4x4x16 slice. The times are simulated.
512 devices in a mesh: dp: 16 (over z), expert: 32 (over y, x, core).
Axes of the slice: x: 4, y: 4, z: 16, core: 2. Of those that a mesh axis runs over, the one named last changes fastest.
Arguments:
- tokens: bfloat16 [65536, 1024], P(('dp', 'expert')), may hold values from -24 to 24
- expert_ids: int32 [65536, 2], P(('dp', 'expert')), may hold values from 0 to 31, all different within a row; in each aligned block of 128 rows (0 to 127, 128 to 255, ...) at most 32 rows name the same one
- route_probs: float32 [65536, 2], P(('dp', 'expert')), may hold values from 0.1 to 1
- w_gate: bfloat16 [32, 1024, 384], P('expert', 'dp'), may hold values from -0.1875 to 0.1875
- w_up: bfloat16 [32, 1024, 384], P('expert', 'dp'), may hold values from -0.1875 to 0.1875
- w_down: bfloat16 [32, 384, 1024], P('expert', None, 'dp'), may hold values from -0.3125 to 0.3125
- grad_out: bfloat16 [65536, 1024], P(('dp', 'expert')), may hold values from -2.5 to 2.5
Outputs:
- mixed_out: bfloat16 [65536, 1024], P(('dp', 'expert'))
- grad_tokens: bfloat16 [65536, 1024], P(('dp', 'expert'))
- grad_probs: float32 [65536, 2], P(('dp', 'expert'))
- grad_w_gate: bfloat16 [32, 1024, 384], P('expert', 'dp')
- grad_w_up: bfloat16 [32, 1024, 384], P('expert', 'dp')
- grad_w_down: bfloat16 [32, 384, 1024], P('expert', None, 'dp')
Inputs may be any that keep to these rules, and one draw needn't show every extreme that they name: `expert_ids`: each row names 2 different experts. Within the rows of one device no expert is named by more than 32 rows, and in every draw some expert is named by exactly 32 rows of some device.
All inputs are finite; a program needn't handle non-finite values.
Results may differ from a plain program's by a relative error of at most 0.017.
Values may be sent and summed in bfloat16 or wider, within the bound.
No kernel may reach another device: no remote copies, remote signals or barrier semaphores. Data moves between devices by JAX's collectives and lax.ppermute only.
A program may use at most 128 MiB of HBM per device.

v0:
```python
import jax
import jax.numpy as jnp
from jax import lax
from jax.sharding import PartitionSpec as P


def route_slots(expert_ids, experts):
    flat_ids = expert_ids.reshape(-1)
    onehot = (flat_ids[:, None] == jnp.arange(experts, dtype=jnp.int32)[None, :]).astype(jnp.int32)
    before = jnp.cumsum(onehot, axis=0) - onehot
    slot_of = jnp.sum(before * onehot, axis=1)
    return (flat_ids, slot_of)


def contract_rows(left_op, right_op):
    return lax.dot_general(
        left_op, right_op, (((0,), (0,)), ((), ())), preferred_element_type=jnp.float32
    )


def contract_cols(left_op, right_op):
    return lax.dot_general(
        left_op, right_op, (((1,), (1,)), ((), ())), preferred_element_type=jnp.float32
    )


def shards(tokens, expert_ids, route_probs, w_gate, w_up, w_down, grad_out):
    senders = lax.axis_size("expert")
    tok_rows, model_width = tokens.shape
    top_count = expert_ids.shape[1]
    hidden_width = w_gate.shape[2]
    capacity = min(tok_rows, 4 * tok_rows * top_count // senders)
    total_rows = senders * capacity
    flat_ids, slot_of = route_slots(expert_ids, senders)
    packed = jnp.concatenate([w_gate[0], w_up[0], w_down[0].T], axis=1)
    whole = lax.all_gather(packed[None], "dp", axis=1, tiled=True)[0]
    gate_up = whole[:, : 2 * hidden_width]
    down_t = whole[:, 2 * hidden_width :]
    grad_wide = grad_out.astype(jnp.float32)
    scaled = (
        (route_probs.T[:, :, None] * grad_wide[None])
        .astype(jnp.bfloat16)
        .reshape(tok_rows * top_count, model_width)
    )
    base = flat_ids * (2 * capacity) + slot_of
    slots = jnp.arange(2 * total_rows, dtype=jnp.int32)[:, None]
    pairs = base.reshape(tok_rows, top_count)
    pick_tok = (slots == pairs[None, :, 0]) | (slots == pairs[None, :, 1])
    pick_grad = slots == (pairs.T.reshape(-1) + capacity)[None, :]
    chooser = jnp.concatenate([pick_tok, pick_grad], axis=1).astype(jnp.bfloat16)
    sources = jnp.concatenate([tokens, scaled], axis=0)
    outgoing = jnp.dot(chooser, sources, preferred_element_type=jnp.float32).astype(jnp.bfloat16)
    arrived = lax.all_to_all(
        outgoing.reshape(senders, 2 * capacity, model_width),
        "expert",
        split_axis=0,
        concat_axis=0,
        tiled=True,
    )
    arrived, whole = lax.optimization_barrier((arrived, whole))
    slot_rows = arrived[:, :capacity].reshape(total_rows, model_width)
    grad_in = arrived[:, capacity:].reshape(total_rows, model_width)
    both_pre = jnp.dot(slot_rows, gate_up, preferred_element_type=jnp.float32)
    gate_pre = both_pre[:, :hidden_width]
    up_pre = both_pre[:, hidden_width:]
    sigmoid_g = jax.nn.sigmoid(gate_pre)
    activated = gate_pre * sigmoid_g
    hidden = (activated * up_pre).astype(jnp.bfloat16)
    back_hidden = jnp.dot(grad_in, down_t, preferred_element_type=jnp.float32)
    back_gate = (back_hidden * up_pre * sigmoid_g * (1.0 + gate_pre * (1.0 - sigmoid_g))).astype(
        jnp.bfloat16
    )
    back_up = (back_hidden * activated).astype(jnp.bfloat16)
    back_both = jnp.concatenate([back_gate, back_up], axis=1)
    grad_terms = jnp.concatenate(
        [
            contract_rows(slot_rows, back_both).astype(jnp.bfloat16),
            contract_rows(grad_in, hidden).astype(jnp.bfloat16),
        ],
        axis=1,
    )
    summed = lax.psum_scatter(grad_terms, "dp", scatter_dimension=0, tiled=True)
    expert_out = contract_cols(hidden, down_t).astype(jnp.bfloat16)
    back_rows = contract_cols(back_both, gate_up).astype(jnp.bfloat16)
    leaving = jnp.concatenate(
        [
            expert_out.reshape(senders, capacity, model_width),
            back_rows.reshape(senders, capacity, model_width),
        ],
        axis=1,
    )
    back_home = lax.all_to_all(leaving, "expert", split_axis=0, concat_axis=0, tiled=True)
    back_home, summed = lax.optimization_barrier((back_home, summed))
    own_place = (flat_ids * capacity + slot_of).reshape(tok_rows, top_count).T.reshape(-1)
    taker = (
        (jnp.arange(total_rows, dtype=jnp.int32)[None, :] == own_place[:, None])
        .astype(jnp.bfloat16)
        .reshape(tok_rows * top_count, senders, capacity)
    )
    picked, back_picked = (
        lax.dot_general(
            taker,
            back_home[:, half * capacity : (half + 1) * capacity],
            (((1, 2), (0, 1)), ((), ())),
            preferred_element_type=jnp.float32,
        ).reshape(top_count, tok_rows, model_width)
        for half in (0, 1)
    )
    probs_k = route_probs.T[:, :, None]
    mixed_out = jnp.sum(probs_k * picked, axis=0).astype(jnp.bfloat16)
    grad_probs = jnp.sum(grad_wide[None] * picked, axis=2).T
    grad_tokens = jnp.sum(back_picked.astype(jnp.float32), axis=0).astype(jnp.bfloat16)
    grad_w_gate = summed[:, :hidden_width][None]
    grad_w_up = summed[:, hidden_width : 2 * hidden_width][None]
    grad_w_down = summed[:, 2 * hidden_width :].T[None]
    return (mixed_out, grad_tokens, grad_probs, grad_w_gate, grad_w_up, grad_w_down)


def solution(mesh):
    placed = (
        P(("dp", "expert"), None),
        P(("dp", "expert"), None),
        P(("dp", "expert"), None),
        P("expert", "dp", None),
        P("expert", "dp", None),
        P("expert", None, "dp"),
        P(("dp", "expert"), None),
    )
    return jax.shard_map(
        shards,
        mesh=mesh,
        in_specs=placed,
        out_specs=(
            P(("dp", "expert"), None),
            P(("dp", "expert"), None),
            P(("dp", "expert"), None),
            P("expert", "dp", None),
            P("expert", "dp", None),
            P("expert", None, "dp"),
        ),
        check_vma=False,
    )
```

profile of v0, /device:TPU:20, one launch (start us, length us, event | category | flops | bytes accessed | tf_op | source)
XLA Modules:
  0.0 189.0 jit_solution(14123776317597047402)
XLA Ops:
  7.2 1.6 pad_maximum_fusion.5
  8.9 0.8 copy.51
  9.9 0.6 reduce-window.6
  10.5 0.2 slice_reduce_fusion
  10.9 0.1 reduce_sum.39
  11.1 0.7 add_bitcast_fusion.1
  11.8 0.3 iota_compare_fusion
  12.1 0.2 fusion.27
  12.4 1.0 convert_element_type.48
  13.5 2.3 %convolution_convert_fusion = bf16[2048,1024]{1,0:T(8,128)(2,1)S(1)} fusion(pred[2048,256]{1,0:T(32,128)(4,1)S(1)} %iota_compare_fusion, pred[2048,128]{1,0:T(32,128)(4,1)S(1)} %fusion.27, bf16[256,1024]{1,0:T(8,128)(2,1)S(1)} %fusion.26, bf16[128,1024]{1,0:T(8,128)(2,1)S(1)} %copy-done.3), kind=kOutput, calls=%fused_computation.1 | convolution fusion | flops 1615069184 | bytes 5767168 | tf_op jit(solution)/shard_map/dot_general | solution.py:52
  15.9 56.1 %all_to_all.10 = bf16[32,64,1024]{2,1,0:T(8,128)(2,1)} all-to-all(bf16[32,64,1024]{2,1,0:T(8,128)(2,1)S(1)} %bitcast.84), channel_id=1, replica_groups=mesh['dp'=16,'expert'=32] {'expert'}, dimensions={0} | all-to-all | bytes 8388608 | tf_op jit(solution)/shard_map/all_to_all | solution.py:53
  72.0 17.1 %all-gather.3.cloned.1.call-done = bf16[1024,1152]{1,0:T(8,128)(2,1)} async-done(((bf16[64,1152]{1,0:T(8,128)(2,1)}), bf16[1024,1152]{1,0:T(8,128)(2,1)}) %all-gather.3.cloned.1.call-update) | async-done | bytes 2359312 | tf_op jit(solution)/shard_map/all_gather | solution.py:36
  89.0 2.8 %fusion.46 = (bf16[32,32,1024]{2,1,0:T(8,128)(2,1)S(1)}, bf16[32,32,1024]{2,1,0:T(8,128)(2,1)S(1)}) fusion(bf16[32,64,1024]{2,1,0:T(8,128)(2,1)} %all_to_all.10), kind=kLoop, calls=%fused_computation.71 | loop fusion | bytes 8388608 | tf_op jit(solution)/shard_map/slice | solution.py:61
  92.0 1.9 %fusion.11 = f32[1024,768]{0,1:T(8,128)S(1)} fusion(bf16[1024,1024]{1,0:T(8,128)(2,1)S(1)} %bitcast.85, bf16[1024,1152]{1,0:T(8,128)(2,1)S(1)} %copy-done.1), kind=kOutput, calls=%fused_computation.24 | convolution fusion | flops 1610612736 | bytes 6815744 | tf_op jit(solution)/shard_map/dot_general | solution.py:63
  93.9 1.7 multiply_convert_fusion.1
  95.6 1.0 convolution_convert_fusion.4
  96.7 0.3 copy-done.7
  97.0 1.8 convolution_convert_fusion.3
  98.8 0.2 pad_maximum_fusion.1
  99.0 2.5 %copy.61 = bf16[1024,1152]{1,0:T(8,128)(2,1)} copy(bf16[1024,1152]{0,1:T(8,128)(2,1)S(1)} %pad_maximum_fusion.1) | data formatting | bytes 4718592
  101.6 1.6 copy-done.2
  103.2 2.6 %convolution_convert_fusion.1 = bf16[1024,1024]{1,0:T(8,128)(2,1)S(1)} fusion(bf16[1024,384]{0,1:T(8,128)(2,1)} %copy-done.4, bf16[1024,1152]{1,0:T(8,128)(2,1)S(1)} %copy-done.2), kind=kOutput, calls=%fused_computation.13 | convolution fusion | flops 806354944 | bytes 3670016 | tf_op jit(solution)/shard_map/dot_general | solution.py:22
  105.8 1.9 convolution_convert_fusion.2
  107.7 2.7 %pad_maximum_fusion = bf16[32,64,1024]{2,1,0:T(8,128)(2,1)} fusion(bf16[32,32,1024]{2,1,0:T(8,128)(2,1)S(1)} %bitcast.90, bf16[32,32,1024]{2,1,0:T(8,128)(2,1)S(1)} %bitcast.89), kind=kLoop, calls=%fused_computation | loop fusion | flops 8388608 | bytes 8388608 | tf_op jit(solution)/shard_map/concatenate | solution.py:85
  110.4 7.4 %all-to-all-start.1 = ((bf16[32,64,1024]{2,1,0:T(8,128)(2,1)}), bf16[32,64,1024]{2,1,0:T(8,128)(2,1)}, u32[]{:S(2)}, u32[]{:S(2)}) async-start(bf16[32,64,1024]{2,1,0:T(8,128)(2,1)} %pad_maximum_fusion), calls=%async_computation.1 | async-start | bytes 8388608 | tf_op jit(solution)/shard_map/all_to_all | solution.py:92
  117.8 54.2 %reduce-scatter.4.cloned.1.call-done = bf16[64,1152]{1,0:T(8,128)(2,1)} async-done(((bf16[1024,1152]{1,0:T(8,128)(2,1)}), bf16[64,1152]{1,0:T(8,128)(2,1)}) %reduce-scatter.4.cloned.1.call-update) | async-done | bytes 147472
  172.0 1.1 copy.62
  173.2 0.7 copy.56
  173.9 0.7 copy.57
  174.6 0.7 copy.58
  175.4 3.3 %fusion.21 = bf16[128,1024]{1,0:T(8,128)(2,1)} fusion(bf16[32,64,1024]{2,1,0:T(8,128)(2,1)} %all-to-all-done.1, s32[2,128]{1,0:T(2,128)S(1)} %get-tuple-element.54, s32[32,32]{1,0:T(8,128)S(1)} %multiply_add_fusion), kind=kOutput, calls=%fused_computation.30 | convolution fusion | flops 537264128 | bytes 2364416 | tf_op jit(solution)/shard_map/dot_general | solution.py:101
  178.7 3.4 %multiply_reduce_fusion = (f32[2,128]{1,0:T(2,128)}, bf16[128,1024]{1,0:T(8,128)(2,1)}) fusion(f32[128,1024]{1,0:T(8,128)S(1)} %convert_element_type.48, f32[2,128]{1,0:T(2,128)S(1)} %bitcast.95, bf16[32,64,1024]{2,1,0:T(8,128)(2,1)} %all-to-all-done.1, s32[2,128]{1,0:T(2,128)S(1)} %get-tuple-element.54, s32[32,32]{1,0:T(8,128)S(1)} %multiply_add_fusion), kind=kOutput, calls=%fused_computation.33 | convolution fusion | flops 538050304 | bytes 2890752 | tf_op jit(solution)/shard_map/dot_general | solution.py:101
  (32 shorter events, 1.0 us)
Async XLA Ops:
  7.2 6.2 %copy-start = (f32[128,2]{0,1:T(2,128)S(1)}, f32[128,2]{0,1:T(2,128)}, u32[]{:S(2)}) copy-start(f32[128,2]{0,1:T(2,128)} %param.9) | copy-start | bytes 3076
  7.2 6.3 %copy-start.3 = (bf16[128,1024]{1,0:T(8,128)(2,1)S(1)}, bf16[128,1024]{1,0:T(8,128)(2,1)}, u32[]{:S(2)}) copy-start(bf16[128,1024]{1,0:T(8,128)(2,1)} %param.7) | copy-start | bytes 786436
  7.2 81.8 %all-gather.3.cloned.1.call-start = ((), (), s32[]{:S(2)}) async-start(), calls=%async_computation.3 | async-start | bytes 2506752 | tf_op jit(solution)/shard_map/all_gather | solution.py:36
  8.8 163.2 %reduce-scatter.4.cloned.1.call-start = ((), (), s32[]{:S(2)}) async-start(), calls=%async_computation.4 | async-start | bytes 2506752
  89.0 2.9 %copy-start.1 = (bf16[1024,1152]{1,0:T(8,128)(2,1)S(1)}, bf16[1024,1152]{1,0:T(8,128)(2,1)}, u32[]{:S(2)}) copy-start(bf16[1024,1152]{1,0:T(8,128)(2,1)} %all-gather.3.cloned.1.call-done) | copy-start | bytes 7077892
  95.6 1.0 copy-start.4
  95.6 1.1 copy-start.5
  95.6 1.4 copy-start.7
  101.5 1.7 copy-start.2
  103.2 2.6 %copy-start.6 = (bf16[1024,384]{0,1:T(8,128)(2,1)S(1)}, bf16[1024,384]{0,1:T(8,128)(2,1)}, u32[]{:S(2)}) copy-start(bf16[1024,384]{0,1:T(8,128)(2,1)} %copy-done.5) | copy-start | bytes 2359300
  103.2 2.6 %copy-start.8 = (bf16[1024,384]{0,1:T(8,128)(2,1)S(1)}, bf16[1024,384]{0,1:T(8,128)(2,1)}, u32[]{:S(2)}) copy-start(bf16[1024,384]{0,1:T(8,128)(2,1)} %copy-done.7) | copy-start | bytes 2359300
  110.4 62.8 %all-to-all-start.1 = ((bf16[32,64,1024]{2,1,0:T(8,128)(2,1)}), bf16[32,64,1024]{2,1,0:T(8,128)(2,1)}, u32[]{:S(2)}, u32[]{:S(2)}) async-start(bf16[32,64,1024]{2,1,0:T(8,128)(2,1)} %pad_maximum_fusion), calls=%async_computation.1 | async-start | bytes 8388608 | tf_op jit(solution)/shard_map/all_to_all | solution.py:92
Sparse Core Ops, SparseCore 0:
  10.7 78.3 all-gather.2
  101.7 70.3 reduce-scatter.3
where the time goes:
time: 189 us
  waiting for transfers between devices  71.4 us (38%)
  blocking collectives  56.1 us (30%)
  matrix products  19.9 us (11%)
  between operations  14.3 us (8%)
  local copies, waits for them, and re-layouts  12.2 us (6%)
  other arithmetic  7.57 us (4%)
  starting transfers between devices  7.52 us (4%)
    all_to_all x1, blocking collectives, shards(): lax.all_to_all(outgoing.reshape(senders, 2 * capacity, model_width), 'exp...  56.1 us
    unnamed x3, waiting for transfers between devices  54.3 us
    all_gather x1, waiting for transfers between devices, shards(): whole = lax.all_gather(packed[None], 'dp', axis=1, tiled=True)[0]  17.1 us
    unnamed x23, local copies, waits for them, and re-layouts  7.6 us
    all_to_all x1, starting transfers between devices, shards(): lax.all_to_all(leaving, 'expert', split_axis=0, concat_axis=0, tiled=True)  7.44 us
    dot_general x2, matrix products, shards(): lax.dot_general(taker, back_home[:, half * capacity:(half + 1) * capacity...  6.76 us
    dot_general x2, matrix products, contract_cols(): lax.dot_general(left_op, right_op, (((1,), (1,)), ((), ())), preferred_el...  4.42 us
  transfers between devices with their start and end apart: 3, of which 2 were waited for; matrix products, arithmetic and copies ran while one was open for 8% of the time, Pallas kernels for 0%

commit v1 on v0

--- a/solution.py
+++ b/solution.py
@@ -33,7 +33,9 @@
     total_rows = senders * capacity
     flat_ids, slot_of = route_slots(expert_ids, senders)
     packed = jnp.concatenate([w_gate[0], w_up[0], w_down[0].T], axis=1)
-    whole = lax.all_gather(packed[None], "dp", axis=1, tiled=True)[0]
+    whole = jnp.concatenate(
+        lax.all_to_all(jnp.stack([packed[None]] * lax.axis_size("dp")), "dp", 0, 0), axis=1
+    )[0]
     gate_up = whole[:, : 2 * hidden_width]
     down_t = whole[:, 2 * hidden_width :]
     grad_wide = grad_out.astype(jnp.float32)

time: 189 us -> 296 us (1.57)
  the two profiles are of different devices: /device:TPU:20 before, /device:TPU:2 now
where the time goes in v1:
time: 296 us; the launch traced here: 295 us
  blocking collectives  121 us (41%)
  waiting for transfers between devices  104 us (35%)
  matrix products  21.9 us (7%)
  starting transfers between devices  15.7 us (5%)
  between operations  14.3 us (5%)
  local copies, waits for them, and re-layouts  13.2 us (4%)
  other arithmetic  6.02 us (2%)
    all_to_all x1, blocking collectives, shards(): lax.all_to_all(jnp.stack([packed[None]] * lax.axis_size('dp')), 'dp', 0, 0)  121 us
    unnamed x2, waiting for transfers between devices  52.2 us
    all_to_all x1, waiting for transfers between devices, shards(): lax.all_to_all(outgoing.reshape(senders, 2 * capacity, model_width), 'exp...  51.4 us
    all_to_all x1, starting transfers between devices, shards(): lax.all_to_all(outgoing.reshape(senders, 2 * capacity, model_width), 'exp...  10.5 us
    unnamed x29, local copies, waits for them, and re-layouts  7.52 us
    dot_general x2, matrix products, shards(): lax.dot_general(taker, back_home[:, half * capacity:(half + 1) * capacity...  6.76 us
  transfers between devices with their start and end apart: 3, of which 2 were waited for; matrix products, arithmetic and copies ran while one was open for 3% of the time, Pallas kernels for 0%

profile of v1, /device:TPU:2, one launch (start us, length us, event | category | flops | bytes accessed | tf_op | source)
XLA Modules:
  0.0 295.3 jit_solution(1000982617015560960)
XLA Ops:
  7.2 0.8 copy.51
  8.3 0.6 reduce-window.6
  8.9 0.2 slice_reduce_fusion
  9.4 0.7 add_bitcast_fusion.1
  10.2 0.3 iota_compare_fusion
  10.5 1.0 convert_element_type.48
  11.5 0.2 fusion.27
  11.9 4.3 %convolution_convert_fusion = bf16[2048,1024]{1,0:T(8,128)(2,1)} fusion(pred[2048,256]{1,0:T(32,128)(4,1)S(1)} %iota_compare_fusion, pred[2048,128]{1,0:T(32,128)(4,1)S(1)} %fusion.27, bf16[256,1024]{1,0:T(8,128)(2,1)S(1)} %fusion.26, bf16[128,1024]{1,0:T(8,128)(2,1)S(1)} %copy-done.6), kind=kOutput, calls=%fused_computation.1 | convolution fusion | flops 1615069184 | bytes 5767168 | tf_op jit(solution)/shard_map/dot_general | solution.py:54
  16.2 10.5 %all-to-all-start = ((bf16[32,64,1024]{2,1,0:T(8,128)(2,1)}), bf16[32,64,1024]{2,1,0:T(8,128)(2,1)}, u32[]{:S(2)}, u32[]{:S(2)}) async-start(bf16[32,64,1024]{2,1,0:T(8,128)(2,1)} %bitcast.85), calls=%async_computation | async-start | bytes 8388608 | tf_op jit(solution)/shard_map/all_to_all | solution.py:55
  26.8 51.4 %all-to-all-done = bf16[32,64,1024]{2,1,0:T(8,128)(2,1)} async-done(((bf16[32,64,1024]{2,1,0:T(8,128)(2,1)}), bf16[32,64,1024]{2,1,0:T(8,128)(2,1)}, u32[]{:S(2)}, u32[]{:S(2)}) %all-to-all-start) | async-done | bytes 4194336 | tf_op jit(solution)/shard_map/all_to_all | solution.py:55
  78.2 0.3 stack.3
  78.5 120.7 %all_to_all.15 = bf16[16,1,64,1152]{3,2,1,0:T(8,128)(2,1)S(1)} all-to-all(bf16[16,1,64,1152]{3,2,1,0:T(8,128)(2,1)S(1)} %stack.3), channel_id=1, replica_groups=mesh['dp'=16,'expert'=32] {'dp'}, dimensions={0} | all-to-all | bytes 4718592 | tf_op jit(solution)/shard_map/all_to_all | solution.py:37
  199.1 3.5 %fusion.46 = (bf16[32,32,1024]{2,1,0:T(8,128)(2,1)S(1)}, bf16[32,32,1024]{2,1,0:T(8,128)(2,1)S(1)}) fusion(bf16[32,64,1024]{2,1,0:T(8,128)(2,1)} %all-to-all-done), kind=kLoop, calls=%fused_computation.71 | loop fusion | bytes 8388608 | tf_op jit(solution)/shard_map/slice | solution.py:63
  202.7 1.9 fusion.11
  204.6 1.7 multiply_convert_fusion.1
  206.3 1.0 convolution_convert_fusion.4
  207.4 0.3 copy-done.10
  207.7 1.8 convolution_convert_fusion.3
  209.5 0.2 pad_maximum_fusion.1
  209.7 2.5 copy.61
  212.2 1.6 copy-done.1
  213.9 2.6 convolution_convert_fusion.1
  216.5 1.9 convolution_convert_fusion.2
  218.3 2.7 pad_maximum_fusion
  221.0 5.2 %all-to-all-start.2 = ((bf16[32,64,1024]{2,1,0:T(8,128)(2,1)}), bf16[32,64,1024]{2,1,0:T(8,128)(2,1)}, u32[]{:S(2)}, u32[]{:S(2)}) async-start(bf16[32,64,1024]{2,1,0:T(8,128)(2,1)} %pad_maximum_fusion), calls=%async_computation.2 | async-start | bytes 8388608 | tf_op jit(solution)/shard_map/all_to_all | solution.py:94
  226.2 52.1 %reduce-scatter.4.cloned.1.call-done = bf16[64,1152]{1,0:T(8,128)(2,1)} async-done(((bf16[1024,1152]{1,0:T(8,128)(2,1)}), bf16[64,1152]{1,0:T(8,128)(2,1)}) %reduce-scatter.4.cloned.1.call-update) | async-done | bytes 147472
  278.4 1.1 copy.62
  279.5 0.7 copy.56
  280.3 0.7 copy.57
  281.0 0.7 copy.58
  281.7 3.3 %fusion.21 = bf16[128,1024]{1,0:T(8,128)(2,1)} fusion(bf16[32,64,1024]{2,1,0:T(8,128)(2,1)} %all-to-all-done.2, s32[2,128]{1,0:T(2,128)S(1)} %get-tuple-element.54, s32[32,32]{1,0:T(8,128)S(1)} %multiply_add_fusion), kind=kOutput, calls=%fused_computation.30 | convolution fusion | flops 537264128 | bytes 2364416 | tf_op jit(solution)/shard_map/dot_general | solution.py:103
  285.0 3.4 %multiply_reduce_fusion = (f32[2,128]{1,0:T(2,128)}, bf16[128,1024]{1,0:T(8,128)(2,1)}) fusion(f32[128,1024]{1,0:T(8,128)S(1)} %convert_element_type.48, f32[2,128]{1,0:T(2,128)S(1)} %bitcast.100, bf16[32,64,1024]{2,1,0:T(8,128)(2,1)} %all-to-all-done.2, s32[2,128]{1,0:T(2,128)S(1)} %get-tuple-element.54, s32[32,32]{1,0:T(8,128)S(1)} %multiply_add_fusion), kind=kOutput, calls=%fused_computation.33 | convolution fusion | flops 538050304 | bytes 2890752 | tf_op jit(solution)/shard_map/dot_general | solution.py:103
  (38 shorter events, 1.0 us)
Async XLA Ops:
  7.2 4.6 %copy-start.5 = (f32[128,2]{0,1:T(2,128)S(1)}, f32[128,2]{0,1:T(2,128)}, u32[]{:S(2)}) copy-start(f32[128,2]{0,1:T(2,128)} %param.9) | copy-start | bytes 3076
  7.2 4.7 %copy-start.6 = (bf16[128,1024]{1,0:T(8,128)(2,1)S(1)}, bf16[128,1024]{1,0:T(8,128)(2,1)}, u32[]{:S(2)}) copy-start(bf16[128,1024]{1,0:T(8,128)(2,1)} %param.7) | copy-start | bytes 786436
  16.2 10.5 %copy-start.2 = (bf16[1,384,64]{1,2,0:T(8,128)(2,1)S(1)}, bf16[1,384,64]{1,2,0:T(8,128)(2,1)}, u32[]{:S(2)}) copy-start(bf16[1,384,64]{1,2,0:T(8,128)(2,1)} %param.12) | copy-start | bytes 147460
  16.2 10.5 %copy-start.3 = (bf16[1,64,384]{2,1,0:T(8,128)(2,1)S(1)}, bf16[1,64,384]{2,1,0:T(8,128)(2,1)}, u32[]{:S(2)}) copy-start(bf16[1,64,384]{2,1,0:T(8,128)(2,1)} %param.11) | copy-start | bytes 147460
  16.2 10.6 %copy-start.4 = (bf16[1,64,384]{2,1,0:T(8,128)(2,1)S(1)}, bf16[1,64,384]{2,1,0:T(8,128)(2,1)}, u32[]{:S(2)}) copy-start(bf16[1,64,384]{2,1,0:T(8,128)(2,1)} %param.10) | copy-start | bytes 147460
  16.2 62.0 %all-to-all-start = ((bf16[32,64,1024]{2,1,0:T(8,128)(2,1)}), bf16[32,64,1024]{2,1,0:T(8,128)(2,1)}, u32[]{:S(2)}, u32[]{:S(2)}) async-start(bf16[32,64,1024]{2,1,0:T(8,128)(2,1)} %bitcast.85), calls=%async_computation | async-start | bytes 8388608 | tf_op jit(solution)/shard_map/all_to_all | solution.py:55
  26.7 251.7 %reduce-scatter.4.cloned.1.call-start = ((), (), s32[]{:S(2)}) async-start(), calls=%async_computation.4 | async-start | bytes 2506752
  199.1 5.4 %copy-start = (bf16[16,1,64,1152]{3,2,1,0:T(8,128)(2,1)}, bf16[16,1,64,1152]{3,2,1,0:T(8,128)(2,1)S(1)}, u32[]{:S(2)}) copy-start(bf16[16,1,64,1152]{3,2,1,0:T(8,128)(2,1)S(1)} %all_to_all.15) | copy-start | bytes 7077892
  206.3 1.0 copy-start.7
  206.3 1.1 copy-start.8
  206.3 1.4 copy-start.10
  212.2 1.7 copy-start.1
  213.9 2.6 copy-start.9
  213.9 2.6 copy-start.11
  221.0 58.5 %all-to-all-start.2 = ((bf16[32,64,1024]{2,1,0:T(8,128)(2,1)}), bf16[32,64,1024]{2,1,0:T(8,128)(2,1)}, u32[]{:S(2)}, u32[]{:S(2)}) async-start(bf16[32,64,1024]{2,1,0:T(8,128)(2,1)} %pad_maximum_fusion), calls=%async_computation.2 | async-start | bytes 8388608 | tf_op jit(solution)/shard_map/all_to_all | solution.py:94
Sparse Core Ops, SparseCore 0:
  212.4 65.9 reduce-scatter.3
